TPU v7x, 256 devices: a whole 4x4x8 slice. The times are simulated.
256 devices in a mesh: svc: 32 (over y_lo, z, core), tm: 8 (over y_hi, x).
Axes of the slice: x: 4, y: 4 (y_hi: 2, y_lo: 2; y = y_hi * 2 + y_lo), z: 8, core: 2. Of those that a mesh axis runs over, the one named last changes fastest.
Arguments:
- metrics: bfloat16 [8192, 4096], P('svc', 'tm'), may hold values from -15 to 15
- band_starts: int32 [4], replicated, may hold values from 1 to 2015
Outputs:
- cross: bfloat16 [4, 2, 8192, 8192], P(None, None, 'svc', 'tm')
- coherence: float32 [4, 8192, 8192], P(None, 'svc', 'tm')
Inputs may be any that keep to these rules, and one draw needn't show every extreme that they name: `band_starts`: each band covers 32 consecutive bins starting at its entry.
All inputs are finite; a program needn't handle non-finite values.
Results may differ from a plain program's by a relative error of at most 0.0066.
Values may be sent and summed in bfloat16 or wider, within the bound.
No kernel may reach another device: no remote copies, remote signals or barrier semaphores. Data moves between devices by JAX's collectives and lax.ppermute only.
A program may use at most 64 MiB of HBM per device.

v0:
```python
import jax
import jax.numpy as jnp
from jax import lax
from jax.sharding import PartitionSpec as P

TLEN = 4096
BANDS = 4
BINS = 32
epsilon = 1e-06


def make_table(minutes, band_starts):
    offsets = jnp.arange(BINS, dtype=jnp.int32)
    freqs = band_starts[:, None] + offsets[None, :]
    phase_index = minutes[:, None, None] * freqs[None, :, :] % TLEN
    phases = 2.0 * jnp.pi / TLEN * phase_index.astype(jnp.float32)
    norm = 1.0 / jnp.sqrt(jnp.float32(TLEN))
    stacked = jnp.stack([jnp.cos(phases) * norm, -jnp.sin(phases) * norm], axis=2)
    return stacked.reshape(minutes.shape[0], BANDS * 2 * BINS).astype(jnp.bfloat16)


def band_products(row_spec, col_spec):
    swapped = jnp.concatenate([row_spec[:, BINS:], -row_spec[:, :BINS]], axis=1)
    dims = (((1,), (1,)), ((), ()))
    real_part = lax.dot_general(row_spec, col_spec, dims, preferred_element_type=jnp.float32) / BINS
    imag_part = lax.dot_general(swapped, col_spec, dims, preferred_element_type=jnp.float32) / BINS
    row_power = jnp.sum(jnp.square(row_spec.astype(jnp.float32)), axis=1) / BINS
    col_power = jnp.sum(jnp.square(col_spec.astype(jnp.float32)), axis=1) / BINS
    coherence = (real_part * real_part + imag_part * imag_part) / (
        (row_power[:, None] + epsilon) * (col_power[None, :] + epsilon)
    )
    cross = jnp.stack([real_part, imag_part], axis=0).astype(jnp.bfloat16)
    return (cross, coherence)


def body(metrics, band_starts):
    row_count = metrics.shape[0]
    local_minutes = metrics.shape[1]
    n_tm = lax.axis_size("tm")
    n_svc = lax.axis_size("svc")
    owners = n_svc // n_tm
    width = BANDS * 2 * BINS
    chunk = width // n_tm
    time_index = lax.axis_index("tm")
    minutes = time_index * local_minutes + jnp.arange(local_minutes, dtype=jnp.int32)
    dft_table = make_table(minutes, band_starts).reshape(local_minutes, n_tm, chunk)
    partial_value = jnp.einsum(
        "nt,tcb->cnb", metrics, dft_table, preferred_element_type=jnp.float32
    )
    piece = lax.psum_scatter(partial_value, "tm", scatter_dimension=0, tiled=True)
    piece = piece.astype(jnp.bfloat16)
    row_chunks = lax.all_gather(piece, "tm", axis=0, tiled=True)
    spectra = jnp.transpose(row_chunks, (1, 0, 2)).reshape(row_count, width)
    perm = []
    for s_src in range(n_svc):
        g_src, r_src = divmod(s_src, owners)
        for t_src in range(n_tm):
            s_dst = t_src * owners + r_src
            t_dst = g_src
            perm.append((s_src * n_tm + t_src, s_dst * n_tm + t_dst))
    moved = lax.ppermute(piece, ("svc", "tm"), perm)
    col_chunks = lax.all_gather(moved, "svc", axis=0, tiled=True)
    columns_panel = (
        col_chunks.reshape(n_tm, owners, row_count, chunk)
        .transpose(1, 2, 0, 3)
        .reshape(owners * row_count, width)
    )
    cross_list = []
    coherence_list = []
    for band in range(BANDS):
        offset = band * 2 * BINS
        row_spec = spectra[:, offset : offset + 2 * BINS]
        col_spec = columns_panel[:, offset : offset + 2 * BINS]
        cross, coherence = band_products(row_spec, col_spec)
        cross_list.append(cross)
        coherence_list.append(coherence)
    return (jnp.stack(cross_list, axis=0), jnp.stack(coherence_list, axis=0))


def solution(mesh):
    return jax.shard_map(
        body,
        mesh=mesh,
        in_specs=(P("svc", "tm"), P()),
        out_specs=(P(None, None, "svc", "tm"), P(None, "svc", "tm")),
        check_vma=False,
    )
```

profile of v0, /device:TPU:1, one launch (start us, length us, event | category | flops | bytes accessed | tf_op | source)
XLA Modules:
  0.0 182.2 jit_solution(15294440074042725612)
XLA Ops:
  7.2 0.0 copy-start
  7.2 0.0 reduce-scatter.2.cloned.1.call-start
  7.2 0.8 iota_add_fusion
  8.0 1.2 multiply_convert_fusion.1
  9.3 0.0 copy-done
  9.3 1.0 convolution_bitcast_fusion
  10.2 0.0 reduce-scatter.2.cloned.1.call-update
  10.3 79.3 %reduce-scatter.2.cloned.1.call-done = f32[1,256,32]{1,2,0:T(8,128)} async-done(((f32[8,256,32]{1,2,0:T(8,128)}), f32[1,256,32]{1,2,0:T(8,128)}) %reduce-scatter.2.cloned.1.call-update) | async-done | bytes 32784 | tf_op jit(solution)/shard_map/reduce_scatter | solution.py:50
  89.6 0.8 convert_element_type.80
  90.3 0.7 collective-permute-start
  91.0 34.3 %all_gather.6 = bf16[8,256,32]{1,2,0:T(8,128)(2,1)S(1)} all-gather(bf16[1,256,32]{1,2,0:T(8,128)(2,1)S(1)} %convert_element_type.80), channel_id=1, replica_groups=mesh['svc'=32,'tm'=8] {'tm'}, dimensions={0}, use_global_device_ids=true | all-gather | bytes 147456 | tf_op jit(solution)/shard_map/all_gather | solution.py:52
  125.4 0.0 collective-permute-done
  125.4 41.4 %all_gather.7 = bf16[32,256,32]{1,2,0:T(8,128)(2,1)S(1)} all-gather(bf16[1,256,32]{1,2,0:T(8,128)(2,1)S(1)} %collective-permute-done), channel_id=1, replica_groups=mesh['svc'=32,'tm'=8] {'svc'}, dimensions={0}, use_global_device_ids=true | all-gather | bytes 540672 | tf_op jit(solution)/shard_map/all_gather | solution.py:62
  166.8 0.4 copy.5
  167.2 0.1 copy.6
  167.3 0.1 multiply_reduce_fusion.3
  167.5 0.3 convolution_multiply_fusion.6
  167.8 0.3 convolution_multiply_fusion.2
  168.1 0.3 convolution_multiply_fusion
  168.4 0.3 convolution_multiply_fusion.4
  168.8 0.4 divide_bitcast_fusion.2
  169.2 0.4 divide_bitcast_fusion
  169.6 0.4 divide_bitcast_fusion.1
  170.1 0.4 divide_bitcast_fusion.3
  170.5 2.3 %pad_maximum_fusion = f32[4,256,1024]{2,1,0:T(8,128)} fusion(f32[1,256,1024]{2,1,0:T(8,128)S(1)} %get-tuple-element.19, f32[1,256,1024]{2,1,0:T(8,128)S(1)} %get-tuple-element.16, f32[1,256,1024]{2,1,0:T(8,128)S(1)} %get-tuple-element.13, f32[1,256,1024]{2,1,0:T(8,128)S(1)} %get-tuple-element.10), kind=kLoop, calls=%fused_computation.1 | loop fusion | flops 3145728 | bytes 8388608 | tf_op jit(solution)/shard_map/stack | solution.py:77
  172.8 2.6 %maximum_maximum_fusion = bf16[4,2,256,1024]{3,2,1,0:T(8,128)(2,1)} fusion(bf16[1,1,256,1024]{3,2,1,0:T(8,128)(2,1)S(1)} %get-tuple-element.21, bf16[1,1,256,1024]{3,2,1,0:T(8,128)(2,1)S(1)} %get-tuple-element.20, bf16[1,1,256,1024]{3,2,1,0:T(8,128)(2,1)S(1)} %get-tuple-element.18, bf16[1,1,256,1024]{3,2,1,0:T(8,128)(2,1)S(1)} %get-tuple-element.17, ...), kind=kLoop, calls=%fused_computation | loop fusion | flops 14680064 | bytes 8388608 | tf_op jit(solution)/shard_map/stack | solution.py:77
  (8 shorter events, 0.1 us)
Async XLA Ops:
  7.2 2.1 %copy-start = (bf16[256,512]{1,0:T(8,128)(2,1)S(1)}, bf16[256,512]{1,0:T(8,128)(2,1)}, u32[]{:S(2)}) copy-start(bf16[256,512]{1,0:T(8,128)(2,1)} %param.2) | copy-start | bytes 786436
  7.2 82.4 %reduce-scatter.2.cloned.1.call-start = ((), (), s32[]{:S(2)}) async-start(), calls=%async_computation.1 | async-start | bytes 294912 | tf_op jit(solution)/shard_map/reduce_scatter | solution.py:50
  90.3 35.0 %collective-permute-start = (bf16[1,256,32]{1,2,0:T(8,128)(2,1)S(1)}, bf16[1,256,32]{1,2,0:T(8,128)(2,1)S(1)}, u32[]{:S(2)}, u32[]{:S(2)}) collective-permute-start(bf16[1,256,32]{1,2,0:T(8,128)(2,1)S(1)} %convert_element_type.80), channel_id=1, source_target_pairs={{0,0},{1,32},{2,64},{3,96},{4,128},{5,160},{6,192},{7,224},{8,8},{... | collective-permute-start | bytes 49160 | tf_op jit(solution)/shard_map/ppermute | solution.py:61
Sparse Core Ops, SparseCore 0:
  12.4 77.0 reduce-scatter.1
where the time goes:
time: 182 us
  waiting for transfers between devices  79.3 us (44%)
  blocking collectives  75.7 us (42%)
  between operations  14.2 us (8%)
  other arithmetic  7.89 us (4%)
  matrix products  3.91 us (2%)
    reduce_scatter x1, waiting for transfers between devices, body(): lax.psum_scatter(partial_value, 'tm', scatter_dimension=0, tiled=True)  79.3 us
    all_gather x1, blocking collectives, body(): col_chunks = lax.all_gather(moved, 'svc', axis=0, tiled=True)  41.4 us
    all_gather x1, blocking collectives, body(): row_chunks = lax.all_gather(piece, 'tm', axis=0, tiled=True)  34.3 us
    another operation x2, other arithmetic, body(): return (jnp.stack(cross_list, axis=0), jnp.stack(coherence_list, axis=0))  4.9 us
  transfers between devices with their start and end apart: 2, of which 1 were waited for; matrix products, arithmetic and copies ran while one was open for 0% of the time, Pallas kernels for 0%

commit v1 on v0

--- a/solution.py
+++ b/solution.py
@@ -49,7 +49,8 @@
     )
     piece = lax.psum_scatter(partial_value, "tm", scatter_dimension=0, tiled=True)
     piece = piece.astype(jnp.bfloat16)
-    row_chunks = lax.all_gather(piece, "tm", axis=0, tiled=True)
+    stack = jnp.stack([piece] * lax.axis_size("tm"))
+    row_chunks = jnp.concatenate(lax.all_to_all(stack, "tm", 0, 0), axis=0)
     spectra = jnp.transpose(row_chunks, (1, 0, 2)).reshape(row_count, width)
     perm = []
     for s_src in range(n_svc):

time: 182 us -> 156 us (0.86)
  blocking collectives: 75.7 us -> 35.4 us
  starting transfers between devices: 0.69 us -> 13.2 us
    all_gather x1 -> x0, blocking collectives: 34.3 us -> none  [body(): row_chunks = lax.all_gather(piece, 'tm', axis=0, tiled=True)]
    all_to_all x0 -> x1, starting transfers between devices: none -> 12.5 us  [body(): row_chunks = jnp.concatenate(lax.all_to_all(stack, 'tm', 0, 0), axis=0)]
    all_gather x1, blocking collectives: 41.4 us -> 35.4 us  [body(): col_chunks = lax.all_gather(moved, 'svc', axis=0, tiled=True)]
  transfers between devices with their start and end apart: 2 -> 3, of which waited for: 1 -> 1; matrix products, arithmetic and copies ran while one was open for 0% -> 1% of each run, Pallas kernels for 0% -> 0%
where the time goes in v1:
time: 156 us
  waiting for transfers between devices  79.3 us (51%)
  blocking collectives  35.4 us (23%)
  between operations  14.2 us (9%)
  starting transfers between devices  13.2 us (8%)
  other arithmetic  8.65 us (6%)
  matrix products  3.91 us (3%)
    reduce_scatter x1, waiting for transfers between devices, body(): lax.psum_scatter(partial_value, 'tm', scatter_dimension=0, tiled=True)  79.3 us
    all_gather x1, blocking collectives, body(): col_chunks = lax.all_gather(moved, 'svc', axis=0, tiled=True)  35.4 us
    all_to_all x1, starting transfers between devices, body(): row_chunks = jnp.concatenate(lax.all_to_all(stack, 'tm', 0, 0), axis=0)  12.5 us
    another operation x2, other arithmetic, body(): return (jnp.stack(cross_list, axis=0), jnp.stack(coherence_list, axis=0))  4.9 us
  transfers between devices with their start and end apart: 3, of which 1 were waited for; matrix products, arithmetic and copies ran while one was open for 1% of the time, Pallas kernels for 0%

profile of v1, /device:TPU:1, one launch (start us, length us, event | category | flops | bytes accessed | tf_op | source)
XLA Modules:
  0.0 155.9 jit_solution(6283673054088697534)
XLA Ops:
  7.2 0.0 copy-start
  7.2 0.0 reduce-scatter.2.cloned.1.call-start
  7.2 0.8 iota_add_fusion
  8.0 1.2 multiply_convert_fusion.1
  9.3 0.0 copy-done
  9.3 1.0 convolution_bitcast_fusion
  10.2 0.0 reduce-scatter.2.cloned.1.call-update
  10.3 79.3 %reduce-scatter.2.cloned.1.call-done = f32[1,256,32]{1,2,0:T(8,128)} async-done(((f32[8,256,32]{1,2,0:T(8,128)}), f32[1,256,32]{1,2,0:T(8,128)}) %reduce-scatter.2.cloned.1.call-update) | async-done | bytes 32784 | tf_op jit(solution)/shard_map/reduce_scatter | solution.py:50
  89.6 0.8 convert_element_type.82
  90.3 0.7 collective-permute-start
  91.0 0.8 convert_bitcast_fusion.8
  91.8 0.7 stack.76
  92.4 12.5 %all-to-all-start = ((bf16[8,1,256,32]{2,3,1,0:T(8,128)(2,1)}), bf16[8,1,256,32]{2,3,1,0:T(8,128)(2,1)S(1)}, u32[]{:S(2)}, u32[]{:S(2)}) async-start(bf16[8,1,256,32]{2,3,1,0:T(8,128)(2,1)} %stack.76), calls=%async_computation.1 | async-start | bytes 262144 | tf_op jit(solution)/shard_map/all_to_all | solution.py:53
  104.9 0.0 collective-permute-done
  104.9 35.4 %all_gather.3 = bf16[32,256,32]{1,2,0:T(8,128)(2,1)S(1)} all-gather(bf16[1,256,32]{1,2,0:T(8,128)(2,1)S(1)} %collective-permute-done), channel_id=1, replica_groups=mesh['svc'=32,'tm'=8] {'svc'}, dimensions={0}, use_global_device_ids=true | all-gather | bytes 540672 | tf_op jit(solution)/shard_map/all_gather | solution.py:63
  140.3 0.4 copy.6
  140.7 0.1 copy.7
  140.8 0.1 multiply_reduce_fusion.3
  141.0 0.0 all-to-all-done
  141.1 0.3 convolution_multiply_fusion.6
  141.4 0.3 convolution_multiply_fusion.2
  141.7 0.3 convolution_multiply_fusion
  142.1 0.3 convolution_multiply_fusion.4
  142.4 0.4 divide_bitcast_fusion.2
  142.8 0.4 divide_bitcast_fusion
  143.2 0.4 divide_bitcast_fusion.1
  143.7 0.4 divide_bitcast_fusion.3
  144.1 2.3 %pad_maximum_fusion = f32[4,256,1024]{2,1,0:T(8,128)} fusion(f32[1,256,1024]{2,1,0:T(8,128)S(1)} %get-tuple-element.19, f32[1,256,1024]{2,1,0:T(8,128)S(1)} %get-tuple-element.16, f32[1,256,1024]{2,1,0:T(8,128)S(1)} %get-tuple-element.13, f32[1,256,1024]{2,1,0:T(8,128)S(1)} %get-tuple-element.10), kind=kLoop, calls=%fused_computation.1 | loop fusion | flops 3145728 | bytes 8388608 | tf_op jit(solution)/shard_map/stack | solution.py:78
  146.4 2.6 %maximum_maximum_fusion = bf16[4,2,256,1024]{3,2,1,0:T(8,128)(2,1)} fusion(bf16[1,1,256,1024]{3,2,1,0:T(8,128)(2,1)S(1)} %get-tuple-element.21, bf16[1,1,256,1024]{3,2,1,0:T(8,128)(2,1)S(1)} %get-tuple-element.20, bf16[1,1,256,1024]{3,2,1,0:T(8,128)(2,1)S(1)} %get-tuple-element.18, bf16[1,1,256,1024]{3,2,1,0:T(8,128)(2,1)S(1)} %get-tuple-element.17, ...), kind=kLoop, calls=%fused_computation | loop fusion | flops 14680064 | bytes 8388608 | tf_op jit(solution)/shard_map/stack | solution.py:78
  (8 shorter events, 0.1 us)
Async XLA Ops:
  7.2 2.1 %copy-start = (bf16[256,512]{1,0:T(8,128)(2,1)S(1)}, bf16[256,512]{1,0:T(8,128)(2,1)}, u32[]{:S(2)}) copy-start(bf16[256,512]{1,0:T(8,128)(2,1)} %param.2) | copy-start | bytes 786436
  7.2 82.4 %reduce-scatter.2.cloned.1.call-start = ((), (), s32[]{:S(2)}) async-start(), calls=%async_computation.2 | async-start | bytes 294912 | tf_op jit(solution)/shard_map/reduce_scatter | solution.py:50
  90.3 14.6 %collective-permute-start = (bf16[1,256,32]{1,2,0:T(8,128)(2,1)S(1)}, bf16[1,256,32]{1,2,0:T(8,128)(2,1)S(1)}, u32[]{:S(2)}, u32[]{:S(2)}) collective-permute-start(bf16[1,256,32]{1,2,0:T(8,128)(2,1)S(1)} %convert_element_type.82), channel_id=1, source_target_pairs={{0,0},{1,32},{2,64},{3,96},{4,128},{5,160},{6,192},{7,224},{8,8},{... | collective-permute-start | bytes 49160 | tf_op jit(solution)/shard_map/ppermute | solution.py:62
  92.4 48.6 %all-to-all-start = ((bf16[8,1,256,32]{2,3,1,0:T(8,128)(2,1)}), bf16[8,1,256,32]{2,3,1,0:T(8,128)(2,1)S(1)}, u32[]{:S(2)}, u32[]{:S(2)}) async-start(bf16[8,1,256,32]{2,3,1,0:T(8,128)(2,1)} %stack.76), calls=%async_computation.1 | async-start | bytes 262144 | tf_op jit(solution)/shard_map/all_to_all | solution.py:53
Sparse Core Ops, SparseCore 0:
  12.4 77.0 reduce-scatter.1
